TPU v7x, 512 devices: a whole 4x4x16 slice. The times are simulated.
512 devices in a mesh: front: 4 (over y), row: 4 (over x), col: 32 (over z, core).
Axes of the slice: x: 4, y: 4, z: 16, core: 2. Of those that a mesh axis runs over, the one named last changes fastest.
Arguments:
- inverse_factor: bfloat16 [4, 1024, 1024], P('front', ('row', 'col')), as said below
- panel: bfloat16 [4, 8192, 1024], P('front', 'row', 'col'), may hold values from -1.1953125 to 1.1953125
- trailing: float32 [4, 8192, 8192], P('front', 'row', 'col'), may hold values from -6 to 6
- extend_map: int32 [4, 512], P('front'), may hold values from 0 to 511, as said below
Outputs:
- parent_update: float32 [4, 4096, 8192], P('front', 'row', 'col')
Inputs may be any that keep to these rules, and one draw needn't show every extreme that they name: Each inverse_factor[f] is upper triangular with positive diagonal. Each row of extend_map is a permutation of 0 to 511, and extend_map[f, q] % (128) == q % 128.
All inputs are finite; a program needn't handle non-finite values.
Results may differ from a plain program's by a relative error of at most 0.0034.
Values may be sent and summed in bfloat16 or wider, within the bound.
No kernel may reach another device: no remote copies, remote signals or barrier semaphores. Data moves between devices by JAX's collectives and lax.ppermute only.
A program may use at most 64 MiB of HBM per device.

v0:
```python
import jax
import jax.numpy as jnp
from jax import lax
from jax.sharding import Mesh
from jax.sharding import PartitionSpec as P


def from_partner(value, axis, distance):
    mask = 2**distance
    pairs = [(source, source ^ mask) for source in range(lax.axis_size(axis))]
    return lax.ppermute(value, axis, pairs)


def outer_rows(left, right):
    return lax.dot_general(
        left, right, (((1,), (1,)), ((), ())), preferred_element_type=jnp.float32
    )


def ring_gather(value, axis, index, n):
    ahead = [(source, (source + 1) % n) for source in range(n)]
    behind = [(source, (source - 1) % n) for source in range(n)]
    held = [value]
    forward = value
    backward = value
    for step in range(1, n):
        if step % 2:
            forward = lax.ppermute(forward, axis, ahead)
            held.append(forward)
        else:
            backward = lax.ppermute(backward, axis, behind)
            held.append(backward)
    offsets = [0] + [(step + 1) // 2 if step % 2 else -(step // 2) for step in range(1, n)]
    by_offset = [None] * n
    for offset, block in zip(offsets, held):
        by_offset[offset % n] = block
    stacked = jnp.stack(by_offset)
    sources = jnp.arange(n, dtype=jnp.int32)
    return stacked[(index - sources) % n]


def inverse_order(target):
    slots = jnp.arange(target.shape[0], dtype=jnp.int32)
    hit = target[None, :] == slots[:, None]
    return jnp.sum(jnp.where(hit, slots[None, :], 0), axis=1, dtype=jnp.int32)


def local(inverse_factor, panel, trailing, extend_map):
    nrow = lax.axis_size("row")
    nz = lax.axis_size("z")
    ncore = lax.axis_size("core")
    ncol = nz * ncore
    group = nrow * ncol
    row_index = lax.axis_index("row")
    col_index = lax.axis_index("z") * ncore + lax.axis_index("core")
    inverse = lax.all_gather(inverse_factor[0], "core", axis=0, tiled=True)
    inverse = lax.all_gather(inverse, "z", axis=0, tiled=True)
    inverse = ring_gather(inverse, "row", row_index, nrow)
    order = inverse.shape[-1]
    inverse = inverse.reshape(order, order)
    columns = lax.all_gather(panel[0], ("z", "core"), axis=1, tiled=True)

    def solve(rows):
        return jnp.dot(rows, inverse, preferred_element_type=jnp.float32).astype(jnp.bfloat16)

    local_trailing = trailing[0]
    rows_here = local_trailing.shape[0]
    cols_here = local_trailing.shape[1]
    share = rows_here // ncol
    piece = solve(lax.dynamic_slice_in_dim(columns, col_index * share, share, 0))
    block_map = extend_map[0]
    nblocks = block_map.shape[0]
    per_class = nblocks // group
    width = rows_here // (ncol * per_class)
    slots_row = jnp.arange(ncol * per_class, dtype=jnp.int32)
    class_row = slots_row // per_class
    depth_row = slots_row % per_class
    source_row = (depth_row * ncol + class_row) * nrow + row_index
    target_row = class_row * per_class + block_map[source_row] // group
    gather_row = inverse_order(target_row)
    slots_col = jnp.arange(nrow * per_class, dtype=jnp.int32)
    class_col = slots_col // per_class
    depth_col = slots_col % per_class
    source_col = (depth_col * ncol + col_index) * nrow + class_col
    target_col = class_col * per_class + block_map[source_col] // group
    gather_col = inverse_order(target_col)
    own_blocks = (
        lax.dynamic_slice_in_dim(gather_col, row_index * per_class, per_class, 0)
        - row_index * per_class
    )
    copies = jnp.tile(own_blocks, nrow)
    piece = piece.reshape(per_class, width, order)[copies].reshape(nrow, share, order)
    col_side = lax.all_to_all(piece, "row", 0, 0, tiled=True).reshape(cols_here, order)
    blocks_col = slots_col[:, None] == gather_col[None, :]
    same = jnp.arange(width)[:, None] == jnp.arange(width)[None, :]
    select_cols = (
        (blocks_col[:, None, :, None] & same[None, :, None, :])
        .reshape(cols_here, cols_here)
        .astype(jnp.float32)
    )
    solved = solve(columns)
    member = lax.axis_index("front") % 2
    half = rows_here // 2
    half_blocks = half // width

    def half_update(which):
        rows = lax.dynamic_slice_in_dim(local_trailing, which * half, half, 0)
        low = lax.dynamic_slice_in_dim(solved, which * half, half, 0)
        rows, low = lax.optimization_barrier((rows, low))
        moved_cols = jnp.dot(
            rows, select_cols, precision=lax.Precision.HIGHEST, preferred_element_type=jnp.float32
        )
        schur = moved_cols - outer_rows(low, col_side)
        blocks = (
            lax.dynamic_slice_in_dim(gather_row, which * half_blocks, half_blocks, 0)
            - which * half_blocks
        )
        return schur.reshape(half_blocks, width, cols_here)[blocks].reshape(half, cols_here)

    outgoing = half_update(1 - member).astype(jnp.bfloat16)
    incoming = from_partner(outgoing, "front", 0)
    keep = half_update(member)
    return (keep + incoming.astype(jnp.float32))[None]


def solution(mesh):
    devices = mesh.devices
    shape = devices.shape
    fine = Mesh(
        devices.reshape(shape[0], shape[1], shape[2] // 2, 2), ("front", "row", "z", "core")
    )
    cols = ("z", "core")
    return jax.shard_map(
        local,
        mesh=fine,
        in_specs=(
            P("front", ("row",) + cols, None),
            P("front", "row", cols),
            P("front", "row", cols),
            P("front", None),
        ),
        out_specs=P("front", "row", cols),
        check_vma=False,
    )
```

profile of v0, /device:TPU:2, one launch (start us, length us, event | category | flops | bytes accessed | tf_op | source)
XLA Modules:
  0.0 133.4 jit_solution(17239717450245742176)
XLA Ops:
  6.5 0.7 all-gather.5.cloned.1.call-update
  7.3 2.0 %all-gather = bf16[1,16,1024]{2,1,0:T(8,128)(2,1)S(1)} all-gather(bf16[1,8,1024]{2,1,0:T(8,128)(2,1)} %param.4), channel_id=2, replica_groups=mesh['front'=4,'row'=4,'z'=16,'core'=2] {'core'}, dimensions={1}, use_global_device_ids=true | all-gather | bytes 49152 | tf_op jit(solution)/shard_map/all_gather | solution.py:56
  9.3 38.4 %all-gather.1 = bf16[1,256,1024]{2,1,0:T(8,128)(2,1)S(1)} all-gather(bf16[1,16,1024]{2,1,0:T(8,128)(2,1)S(1)} %all-gather), channel_id=3, replica_groups=mesh['front'=4,'row'=4,'z'=16,'core'=2] {'z'}, dimensions={1}, use_global_device_ids=true | all-gather | bytes 557056 | tf_op jit(solution)/shard_map/all_gather | solution.py:57
  47.7 3.4 %collective-permute-start = (bf16[256,1024]{1,0:T(8,128)(2,1)S(1)}, bf16[256,1024]{1,0:T(8,128)(2,1)}, u32[]{:S(2)}, u32[]{:S(2)}) collective-permute-start(bf16[256,1024]{1,0:T(8,128)(2,1)S(1)} %bitcast.60), channel_id=1, source_target_pairs={{0,32},{32,64},{64,96},{96,0},{1,33},{33,65},{65,97},{97,1},{2,34}... | collective-permute-start | bytes 1572872 | tf_op jit(solution)/shard_map/ppermute | solution.py:28
  51.1 2.4 %collective-permute-start.2 = (bf16[256,1024]{1,0:T(8,128)(2,1)S(1)}, bf16[256,1024]{1,0:T(8,128)(2,1)}, u32[]{:S(2)}, u32[]{:S(2)}) collective-permute-start(bf16[256,1024]{1,0:T(8,128)(2,1)S(1)} %bitcast.61), channel_id=1, source_target_pairs={{0,96},{32,0},{64,32},{96,64},{1,97},{33,1},{65,33},{97,65},{2,98}... | collective-permute-start | bytes 1572872 | tf_op jit(solution)/shard_map/ppermute | solution.py:31
  53.6 1.3 gather_fusion.3
  54.9 0.7 gather_fusion.1
  55.6 0.1 select_reduce_fusion.1
  55.9 0.1 select_reduce_fusion
  56.0 0.3 broadcast_and_fusion
  56.3 3.3 %collective-permute-done = bf16[256,1024]{1,0:T(8,128)(2,1)} collective-permute-done((bf16[256,1024]{1,0:T(8,128)(2,1)S(1)}, bf16[256,1024]{1,0:T(8,128)(2,1)}, u32[]{:S(2)}, u32[]{:S(2)}) %collective-permute-start) | collective-permute-done | bytes 524320 | tf_op jit(solution)/shard_map/ppermute | solution.py:28
  59.7 3.6 %collective-permute-start.1 = (bf16[256,1024]{1,0:T(8,128)(2,1)}, bf16[256,1024]{1,0:T(8,128)(2,1)}, u32[]{:S(2)}, u32[]{:S(2)}) collective-permute-start(bf16[256,1024]{1,0:T(8,128)(2,1)} %collective-permute-done), channel_id=1, source_target_pairs={{0,32},{32,64},{64,96},{96,0},{1,33},{33,65},{65,97},{97,1},{2,34}... | collective-permute-start | bytes 1572872 | tf_op jit(solution)/shard_map/ppermute | solution.py:28
  63.4 0.9 and.163
  64.3 1.5 %dynamic-slice_bitcast_fusion.2 = (f32[1024,256]{1,0:T(8,128)}, f32[1024,256]{1,0:T(8,128)}) fusion(f32[1,2048,256]{2,1,0:T(8,128)S(1)} %copy-done.3, s32[]{:T(128)S(6)} %select_n.191, s32[]{:T(128)S(6)} %select_n.171), kind=kLoop, calls=%fused_computation.16 | loop fusion | bytes 4194312 | tf_op jit(solution)/shard_map/dynamic_slice | solution.py:107
  65.8 5.2 %collective-permute-done.1 = bf16[256,1024]{1,0:T(8,128)(2,1)} collective-permute-done((bf16[256,1024]{1,0:T(8,128)(2,1)}, bf16[256,1024]{1,0:T(8,128)(2,1)}, u32[]{:S(2)}, u32[]{:S(2)}) %collective-permute-start.1) | collective-permute-done | bytes 524320 | tf_op jit(solution)/shard_map/ppermute | solution.py:28
  71.0 2.9 %pad_maximum_fusion = bf16[4,256,1024]{2,1,0:T(8,128)(2,1)} fusion(bf16[1,256,1024]{2,1,0:T(8,128)(2,1)} %bitcast.4, bf16[1,256,1024]{2,1,0:T(8,128)(2,1)} %bitcast.3, bf16[1,256,1024]{2,1,0:T(8,128)(2,1)} %bitcast.2, bf16[1,256,1024]{2,1,0:T(8,128)(2,1)S(1)} %all-gather.1), kind=kLoop, calls=%fused_computation.9 | loop fusion | flops 3145728 | bytes 4194304 | tf_op jit(solution)/shard_map/stack | solution.py:37
  74.0 2.3 %gather_fusion = bf16[4,256,1024]{2,1,0:T(8,128)(2,1)S(1)} fusion(bf16[4,256,1024]{2,1,0:T(8,128)(2,1)} %pad_maximum_fusion, s32[1024]{0:T(1024)S(1)} %pad_clamp_fusion.5), kind=kCustom, calls=%fused_computation | custom fusion | bytes 4194320 | tf_op jit(solution)/shard_map/gather | solution.py:39
  76.3 12.4 %all-gather.5.cloned.1.call-done = bf16[1,2048,1024]{1,2,0:T(8,128)(2,1)} async-done(((bf16[1,2048,32]{1,2,0:T(8,128)(2,1)}), bf16[1,2048,1024]{1,2,0:T(8,128)(2,1)}) %all-gather.5.cloned.1.call-update) | async-done | bytes 4194320 | tf_op jit(solution)/shard_map/all_gather | solution.py:61
  88.7 1.6 %convolution_convert_fusion = bf16[64,1024]{1,0:T(8,128)(2,1)S(1)} fusion(bf16[1024,1024]{1,0:T(8,128)(2,1)S(1)} %bitcast.53, bf16[1,2048,1024]{1,2,0:T(8,128)(2,1)} %all-gather.5.cloned.1.call-done, s32[]{:T(128)S(6)} %select_n.180), kind=kOutput, calls=%fused_computation.14 | convolution fusion | flops 134283264 | bytes 2490372 | tf_op jit(solution)/shard_map/dot_general | solution.py:64
  90.2 1.4 %gather_fusion.2 = bf16[16,16,1024]{2,1,0:T(8,128)(2,1)} fusion(bf16[4,16,1024]{2,1,0:T(8,128)(2,1)S(1)} %bitcast.58, s32[1024]{0:T(1024)S(1)} %pad_clamp_fusion.3), kind=kCustom, calls=%fused_computation.2 | custom fusion | bytes 1048640 | tf_op jit(solution)/shard_map/gather | solution.py:92
  91.6 4.8 %all-to-all-start = ((bf16[4,64,1024]{2,1,0:T(8,128)(2,1)}), bf16[4,64,1024]{2,1,0:T(8,128)(2,1)S(1)}, u32[]{:S(2)}, u32[]{:S(2)}) async-start(bf16[4,64,1024]{2,1,0:T(8,128)(2,1)} %bitcast.14), calls=%async_computation | async-start | bytes 1048576 | tf_op jit(solution)/shard_map/all_to_all | solution.py:93
  96.4 7.0 %fusion.2 = bf16[1024,2048]{1,0:T(8,128)(2,1)S(1)} fusion(bf16[1024,1024]{1,0:T(8,128)(2,1)S(1)} %bitcast.54, bf16[1,2048,1024]{1,2,0:T(8,128)(2,1)} %all-gather.5.cloned.1.call-done), kind=kOutput, calls=%fused_computation.8 | convolution fusion | flops 4297064448 | bytes 10485760 | tf_op jit(solution)/shard_map/dot_general | solution.py:64
  103.4 1.8 %dynamic-slice_bitcast_fusion = (bf16[1024,1024]{0,1:T(8,128)(2,1)}, bf16[1024,1024]{0,1:T(8,128)(2,1)S(1)}) fusion(bf16[1024,2048]{1,0:T(8,128)(2,1)S(1)} %fusion.2, s32[]{:T(128)S(6)} %select_n.191, s32[]{:T(128)S(6)} %select_n.171), kind=kLoop, calls=%fused_computation.10 | loop fusion | bytes 8388616 | tf_op jit(solution)/shard_map/dynamic_slice | solution.py:108
  105.2 2.5 %fusion.26 = f32[1024,256]{1,0:T(8,128)S(1)} fusion(bf16[1024,1024]{0,1:T(8,128)(2,1)} %get-tuple-element.12, bf16[256,1024]{1,0:T(8,128)(2,1)S(1)} %bitcast.55), kind=kOutput, calls=%fused_computation.87 | convolution fusion | flops 536870912 | bytes 3670016 | tf_op jit(solution)/shard_map/dot_general | solution.py:15
  107.7 0.7 convolution_subtract_fusion
  108.4 1.4 %gather_fusion.5 = bf16[64,16,256]{2,1,0:T(8,128)(2,1)} fusion(bf16[64,16,256]{2,1,0:T(8,128)(2,1)S(1)} %bitcast.59, s32[1024]{0:T(1024)S(1)} %pad_clamp_fusion), kind=kCustom, calls=%fused_computation.5 | custom fusion | bytes 1048832 | tf_op jit(solution)/shard_map/gather | solution.py:118
  109.8 3.6 %collective-permute-start.3 = (bf16[1024,256]{1,0:T(8,128)(2,1)}, bf16[1024,256]{1,0:T(8,128)(2,1)S(1)}, u32[]{:S(2)}, u32[]{:S(2)}) collective-permute-start(bf16[1024,256]{1,0:T(8,128)(2,1)} %bitcast.62), channel_id=1, source_target_pairs={{0,128},{128,0},{256,384},{384,256},{1,129},{129,1},{257,385},{385... | collective-permute-start | bytes 1572872 | tf_op jit(solution)/shard_map/ppermute | solution.py:11
  113.3 0.8 fusion.25
  114.1 0.7 convolution_subtract_fusion.1
  114.8 0.6 gather_fusion.4
  115.4 10.1 %collective-permute-done.3 = bf16[1024,256]{1,0:T(8,128)(2,1)S(1)} collective-permute-done((bf16[1024,256]{1,0:T(8,128)(2,1)}, bf16[1024,256]{1,0:T(8,128)(2,1)S(1)}, u32[]{:S(2)}, u32[]{:S(2)}) %collective-permute-start.3) | collective-permute-done | bytes 524320 | tf_op jit(solution)/shard_map/ppermute | solution.py:11
  125.5 1.1 bitcast_add_fusion
  (28 shorter events, 0.4 us)
Async XLA Ops:
  6.5 47.0 %copy-start = (s32[1,512]{1,0:T(1,128)S(1)}, s32[1,512]{1,0:T(1,128)}, u32[]{:S(2)}) copy-start(s32[1,512]{1,0:T(1,128)} %param.7) | copy-start | bytes 6148
  6.5 57.7 %copy-start.3 = (f32[1,2048,256]{2,1,0:T(8,128)S(1)}, f32[1,2048,256]{2,1,0:T(8,128)}, u32[]{:S(2)}) copy-start(f32[1,2048,256]{2,1,0:T(8,128)} %param.6) | copy-start | bytes 6291460
  6.5 82.1 %all-gather.5.cloned.1.call-start = ((), (), s32[]{:S(2)}) async-start(), calls=%async_computation.1 | async-start | bytes 4325376 | tf_op jit(solution)/shard_map/all_gather | solution.py:61
  47.7 12.0 %collective-permute-start = (bf16[256,1024]{1,0:T(8,128)(2,1)S(1)}, bf16[256,1024]{1,0:T(8,128)(2,1)}, u32[]{:S(2)}, u32[]{:S(2)}) collective-permute-start(bf16[256,1024]{1,0:T(8,128)(2,1)S(1)} %bitcast.60), channel_id=1, source_target_pairs={{0,32},{32,64},{64,96},{96,0},{1,33},{33,65},{65,97},{97,1},{2,34}... | collective-permute-start | bytes 1572872 | tf_op jit(solution)/shard_map/ppermute | solution.py:28
  51.1 14.7 %collective-permute-start.2 = (bf16[256,1024]{1,0:T(8,128)(2,1)S(1)}, bf16[256,1024]{1,0:T(8,128)(2,1)}, u32[]{:S(2)}, u32[]{:S(2)}) collective-permute-start(bf16[256,1024]{1,0:T(8,128)(2,1)S(1)} %bitcast.61), channel_id=1, source_target_pairs={{0,96},{32,0},{64,32},{96,64},{1,97},{33,1},{65,33},{97,65},{2,98}... | collective-permute-start | bytes 1572872 | tf_op jit(solution)/shard_map/ppermute | solution.py:31
  59.7 11.4 %collective-permute-start.1 = (bf16[256,1024]{1,0:T(8,128)(2,1)}, bf16[256,1024]{1,0:T(8,128)(2,1)}, u32[]{:S(2)}, u32[]{:S(2)}) collective-permute-start(bf16[256,1024]{1,0:T(8,128)(2,1)} %collective-permute-done), channel_id=1, source_target_pairs={{0,32},{32,64},{64,96},{96,0},{1,33},{33,65},{65,97},{97,1},{2,34}... | collective-permute-start | bytes 1572872 | tf_op jit(solution)/shard_map/ppermute | solution.py:28
  91.6 13.6 %all-to-all-start = ((bf16[4,64,1024]{2,1,0:T(8,128)(2,1)}), bf16[4,64,1024]{2,1,0:T(8,128)(2,1)S(1)}, u32[]{:S(2)}, u32[]{:S(2)}) async-start(bf16[4,64,1024]{2,1,0:T(8,128)(2,1)} %bitcast.14), calls=%async_computation | async-start | bytes 1048576 | tf_op jit(solution)/shard_map/all_to_all | solution.py:93
  105.2 2.5 %copy-start.2 = (f32[1024,256]{1,0:T(8,128)S(1)}, f32[1024,256]{1,0:T(8,128)}, u32[]{:S(2)}) copy-start(f32[1024,256]{1,0:T(8,128)} %get-tuple-element.11) | copy-start | bytes 3145732
  109.8 4.3 %copy-start.1 = (f32[1024,256]{1,0:T(8,128)S(1)}, f32[1024,256]{1,0:T(8,128)}, u32[]{:S(2)}) copy-start(f32[1024,256]{1,0:T(8,128)} %get-tuple-element.9) | copy-start | bytes 3145732
  109.8 15.7 %collective-permute-start.3 = (bf16[1024,256]{1,0:T(8,128)(2,1)}, bf16[1024,256]{1,0:T(8,128)(2,1)S(1)}, u32[]{:S(2)}, u32[]{:S(2)}) collective-permute-start(bf16[1024,256]{1,0:T(8,128)(2,1)} %bitcast.62), channel_id=1, source_target_pairs={{0,128},{128,0},{256,384},{384,256},{1,129},{129,1},{257,385},{385... | collective-permute-start | bytes 1572872 | tf_op jit(solution)/shard_map/ppermute | solution.py:11
Sparse Core Ops, SparseCore 0:
  9.5 79.1 all-gather.4
where the time goes:
time: 134 us; the launch traced here: 133 us
  blocking collectives  40.4 us (30%)
  waiting for transfers between devices  31.7 us (24%)
  starting transfers between devices  17.8 us (13%)
  between operations  13.7 us (10%)
  matrix products  13.1 us (10%)
  local copies, waits for them, and re-layouts  11.9 us (9%)
  other arithmetic  4.81 us (4%)
    all_gather x1, blocking collectives, local(): inverse = lax.all_gather(inverse, 'z', axis=0, tiled=True)  38.4 us
    all_gather x1, waiting for transfers between devices, local(): columns = lax.all_gather(panel[0], ('z', 'core'), axis=1, tiled=True)  12.4 us
    ppermute x1, waiting for transfers between devices, from_partner(): return lax.ppermute(value, axis, pairs)  10.1 us
    dot_general x2, matrix products, solve(): jnp.dot(rows, inverse, preferred_element_type=jnp.float32)  8.6 us
    ppermute x2, waiting for transfers between devices, ring_gather(): forward = lax.ppermute(forward, axis, ahead)  8.56 us
    ppermute x2, starting transfers between devices, ring_gather(): forward = lax.ppermute(forward, axis, ahead)  6.99 us
    all_to_all x1, starting transfers between devices, local(): lax.all_to_all(piece, 'row', 0, 0, tiled=True).reshape(cols_here, order)  4.78 us
    ppermute x1, starting transfers between devices, from_partner(): return lax.ppermute(value, axis, pairs)  3.55 us
  transfers between devices with their start and end apart: 6, of which 4 were waited for; matrix products, arithmetic and copies ran while one was open for 16% of the time, Pallas kernels for 0%

commit v1 on v0

--- a/solution.py
+++ b/solution.py
@@ -54,7 +54,9 @@
     row_index = lax.axis_index("row")
     col_index = lax.axis_index("z") * ncore + lax.axis_index("core")
     inverse = lax.all_gather(inverse_factor[0], "core", axis=0, tiled=True)
-    inverse = lax.all_gather(inverse, "z", axis=0, tiled=True)
+    inverse = jnp.concatenate(
+        lax.all_to_all(jnp.stack([inverse] * lax.axis_size("z")), "z", 0, 0), axis=0
+    )
     inverse = ring_gather(inverse, "row", row_index, nrow)
     order = inverse.shape[-1]
     inverse = inverse.reshape(order, order)

time: 134 us -> 145 us (1.082)
  the two profiles are of different devices: /device:TPU:2 before, /device:TPU:18 now
where the time goes in v1:
time: 145 us
  waiting for transfers between devices  66 us (46%)
  starting transfers between devices  32.1 us (22%)
  between operations  13.7 us (9%)
  matrix products  13.1 us (9%)
  local copies, waits for them, and re-layouts  12.7 us (9%)
  other arithmetic  4.84 us (3%)
  blocking collectives  2.04 us (1%)
    all_to_all x1, waiting for transfers between devices, local(): lax.all_to_all(jnp.stack([inverse] * lax.axis_size('z')), 'z', 0, 0)  31.5 us
    all_to_all x1, starting transfers between devices, local(): lax.all_to_all(jnp.stack([inverse] * lax.axis_size('z')), 'z', 0, 0)  15.2 us
    ppermute x2, waiting for transfers between devices, ring_gather(): forward = lax.ppermute(forward, axis, ahead)  14.8 us
    ppermute x1, waiting for transfers between devices, from_partner(): return lax.ppermute(value, axis, pairs)  10.8 us
    dot_general x2, matrix products, solve(): jnp.dot(rows, inverse, preferred_element_type=jnp.float32)  8.61 us
    all_gather x1, waiting for transfers between devices, local(): columns = lax.all_gather(panel[0], ('z', 'core'), axis=1, tiled=True)  8.22 us
    ppermute x2, starting transfers between devices, ring_gather(): forward = lax.ppermute(forward, axis, ahead)  6.76 us
    all_to_all x1, starting transfers between devices, local(): lax.all_to_all(piece, 'row', 0, 0, tiled=True).reshape(cols_here, order)  4.86 us
  transfers between devices with their start and end apart: 7, of which 5 were waited for; matrix products, arithmetic and copies ran while one was open for 15% of the time, Pallas kernels for 0%

profile of v1, /device:TPU:18, one launch (start us, length us, event | category | flops | bytes accessed | tf_op | source)
XLA Modules:
  0.0 144.6 jit_solution(10737000693869222942)
XLA Ops:
  6.5 0.7 all-gather.4.cloned.1.call-update
  7.3 2.0 %all-gather = bf16[1,16,1024]{2,1,0:T(8,128)(2,1)S(1)} all-gather(bf16[1,8,1024]{2,1,0:T(8,128)(2,1)} %param.4), channel_id=2, replica_groups=mesh['front'=4,'row'=4,'z'=16,'core'=2] {'core'}, dimensions={1}, use_global_device_ids=true | all-gather | bytes 49152 | tf_op jit(solution)/shard_map/all_gather | solution.py:56
  9.3 0.9 stack.10
  10.2 15.2 %all-to-all-start = ((bf16[16,16,1024]{2,1,0:T(8,128)(2,1)}), bf16[16,16,1024]{2,1,0:T(8,128)(2,1)S(1)}, u32[]{:S(2)}, u32[]{:S(2)}) async-start(bf16[16,16,1024]{2,1,0:T(8,128)(2,1)} %stack.10), calls=%async_computation | async-start | bytes 1048576 | tf_op jit(solution)/shard_map/all_to_all | solution.py:58
  25.4 1.3 gather_fusion.3
  26.7 0.7 gather_fusion.1
  27.9 31.5 %all-to-all-done = bf16[16,16,1024]{2,1,0:T(8,128)(2,1)S(1)} async-done(((bf16[16,16,1024]{2,1,0:T(8,128)(2,1)}), bf16[16,16,1024]{2,1,0:T(8,128)(2,1)S(1)}, u32[]{:S(2)}, u32[]{:S(2)}) %all-to-all-start) | async-done | bytes 524320 | tf_op jit(solution)/shard_map/all_to_all | solution.py:58
  59.4 3.4 %collective-permute-start = (bf16[256,1024]{1,0:T(8,128)(2,1)S(1)}, bf16[256,1024]{1,0:T(8,128)(2,1)}, u32[]{:S(2)}, u32[]{:S(2)}) collective-permute-start(bf16[256,1024]{1,0:T(8,128)(2,1)S(1)} %bitcast.62), channel_id=1, source_target_pairs={{0,32},{32,64},{64,96},{96,0},{1,33},{33,65},{65,97},{97,1},{2,34}... | collective-permute-start | bytes 1572872 | tf_op jit(solution)/shard_map/ppermute | solution.py:28
  62.8 0.3 broadcast_and_fusion
  63.1 2.4 %collective-permute-start.2 = (bf16[256,1024]{1,0:T(8,128)(2,1)S(1)}, bf16[256,1024]{1,0:T(8,128)(2,1)}, u32[]{:S(2)}, u32[]{:S(2)}) collective-permute-start(bf16[256,1024]{1,0:T(8,128)(2,1)S(1)} %bitcast.63), channel_id=1, source_target_pairs={{0,96},{32,0},{64,32},{96,64},{1,97},{33,1},{65,33},{97,65},{2,98}... | collective-permute-start | bytes 1572872 | tf_op jit(solution)/shard_map/ppermute | solution.py:31
  65.6 9.3 %collective-permute-done = bf16[256,1024]{1,0:T(8,128)(2,1)} collective-permute-done((bf16[256,1024]{1,0:T(8,128)(2,1)S(1)}, bf16[256,1024]{1,0:T(8,128)(2,1)}, u32[]{:S(2)}, u32[]{:S(2)}) %collective-permute-start) | collective-permute-done | bytes 524320 | tf_op jit(solution)/shard_map/ppermute | solution.py:28
  74.9 3.4 %collective-permute-start.1 = (bf16[256,1024]{1,0:T(8,128)(2,1)}, bf16[256,1024]{1,0:T(8,128)(2,1)}, u32[]{:S(2)}, u32[]{:S(2)}) collective-permute-start(bf16[256,1024]{1,0:T(8,128)(2,1)} %collective-permute-done), channel_id=1, source_target_pairs={{0,32},{32,64},{64,96},{96,0},{1,33},{33,65},{65,97},{97,1},{2,34}... | collective-permute-start | bytes 1572872 | tf_op jit(solution)/shard_map/ppermute | solution.py:28
  78.4 0.9 and.163
  79.3 1.5 %dynamic-slice_bitcast_fusion.2 = (f32[1024,256]{1,0:T(8,128)}, f32[1024,256]{1,0:T(8,128)}) fusion(f32[1,2048,256]{2,1,0:T(8,128)S(1)} %copy-done.3, s32[]{:T(128)S(6)} %select_n.191, s32[]{:T(128)S(6)} %select_n.171), kind=kLoop, calls=%fused_computation.16 | loop fusion | bytes 4194312 | tf_op jit(solution)/shard_map/dynamic_slice | solution.py:109
  80.8 5.5 %collective-permute-done.1 = bf16[256,1024]{1,0:T(8,128)(2,1)} collective-permute-done((bf16[256,1024]{1,0:T(8,128)(2,1)}, bf16[256,1024]{1,0:T(8,128)(2,1)}, u32[]{:S(2)}, u32[]{:S(2)}) %collective-permute-start.1) | collective-permute-done | bytes 524320 | tf_op jit(solution)/shard_map/ppermute | solution.py:28
  86.3 3.0 %pad_maximum_fusion = bf16[4,256,1024]{2,1,0:T(8,128)(2,1)} fusion(bf16[1,256,1024]{2,1,0:T(8,128)(2,1)} %bitcast.6, bf16[1,256,1024]{2,1,0:T(8,128)(2,1)} %bitcast.5, bf16[1,256,1024]{2,1,0:T(8,128)(2,1)} %bitcast.4, bf16[1,256,1024]{2,1,0:T(8,128)(2,1)S(1)} %bitcast.64), kind=kLoop, calls=%fused_computation.9 | loop fusion | flops 3145728 | bytes 4194304 | tf_op jit(solution)/shard_map/stack | solution.py:37
  89.3 2.3 %gather_fusion = bf16[4,256,1024]{2,1,0:T(8,128)(2,1)S(1)} fusion(bf16[4,256,1024]{2,1,0:T(8,128)(2,1)} %pad_maximum_fusion, s32[1024]{0:T(1024)S(1)} %pad_clamp_fusion.5), kind=kCustom, calls=%fused_computation | custom fusion | bytes 4194320 | tf_op jit(solution)/shard_map/gather | solution.py:39
  91.6 8.2 %all-gather.4.cloned.1.call-done = bf16[1,2048,1024]{1,2,0:T(8,128)(2,1)} async-done(((bf16[1,2048,32]{1,2,0:T(8,128)(2,1)}), bf16[1,2048,1024]{1,2,0:T(8,128)(2,1)}) %all-gather.4.cloned.1.call-update) | async-done | bytes 4194320 | tf_op jit(solution)/shard_map/all_gather | solution.py:63
  99.8 1.6 %convolution_convert_fusion = bf16[64,1024]{1,0:T(8,128)(2,1)S(1)} fusion(bf16[1024,1024]{1,0:T(8,128)(2,1)S(1)} %bitcast.55, bf16[1,2048,1024]{1,2,0:T(8,128)(2,1)} %all-gather.4.cloned.1.call-done, s32[]{:T(128)S(6)} %select_n.180), kind=kOutput, calls=%fused_computation.14 | convolution fusion | flops 134283264 | bytes 2490372 | tf_op jit(solution)/shard_map/dot_general | solution.py:66
  101.4 1.4 gather_fusion.2
  102.7 4.9 %all-to-all-start.1 = ((bf16[4,64,1024]{2,1,0:T(8,128)(2,1)}), bf16[4,64,1024]{2,1,0:T(8,128)(2,1)S(1)}, u32[]{:S(2)}, u32[]{:S(2)}) async-start(bf16[4,64,1024]{2,1,0:T(8,128)(2,1)} %bitcast.16), calls=%async_computation.1 | async-start | bytes 1048576 | tf_op jit(solution)/shard_map/all_to_all | solution.py:95
  107.6 7.0 %fusion.2 = bf16[1024,2048]{1,0:T(8,128)(2,1)S(1)} fusion(bf16[1024,1024]{1,0:T(8,128)(2,1)S(1)} %bitcast.56, bf16[1,2048,1024]{1,2,0:T(8,128)(2,1)} %all-gather.4.cloned.1.call-done), kind=kOutput, calls=%fused_computation.8 | convolution fusion | flops 4297064448 | bytes 10485760 | tf_op jit(solution)/shard_map/dot_general | solution.py:66
  114.6 1.8 %dynamic-slice_bitcast_fusion = (bf16[1024,1024]{0,1:T(8,128)(2,1)}, bf16[1024,1024]{0,1:T(8,128)(2,1)S(1)}) fusion(bf16[1024,2048]{1,0:T(8,128)(2,1)S(1)} %fusion.2, s32[]{:T(128)S(6)} %select_n.191, s32[]{:T(128)S(6)} %select_n.171), kind=kLoop, calls=%fused_computation.10 | loop fusion | bytes 8388616 | tf_op jit(solution)/shard_map/dynamic_slice | solution.py:110
  116.4 2.5 %fusion.26 = f32[1024,256]{1,0:T(8,128)S(1)} fusion(bf16[1024,1024]{0,1:T(8,128)(2,1)} %get-tuple-element.12, bf16[256,1024]{1,0:T(8,128)(2,1)S(1)} %bitcast.57), kind=kOutput, calls=%fused_computation.87 | convolution fusion | flops 536870912 | bytes 3670016 | tf_op jit(solution)/shard_map/dot_general | solution.py:15
  118.9 0.7 convolution_subtract_fusion
  119.6 1.4 gather_fusion.5
  121.0 2.9 %collective-permute-start.3 = (bf16[1024,256]{1,0:T(8,128)(2,1)}, bf16[1024,256]{1,0:T(8,128)(2,1)S(1)}, u32[]{:S(2)}, u32[]{:S(2)}) collective-permute-start(bf16[1024,256]{1,0:T(8,128)(2,1)} %bitcast.65), channel_id=1, source_target_pairs={{0,128},{128,0},{256,384},{384,256},{1,129},{129,1},{257,385},{385... | collective-permute-start | bytes 1572872 | tf_op jit(solution)/shard_map/ppermute | solution.py:11
  123.8 0.8 fusion.25
  124.6 0.7 convolution_subtract_fusion.1
  125.3 0.6 gather_fusion.4
  125.9 10.8 %collective-permute-done.3 = bf16[1024,256]{1,0:T(8,128)(2,1)S(1)} collective-permute-done((bf16[1024,256]{1,0:T(8,128)(2,1)}, bf16[1024,256]{1,0:T(8,128)(2,1)S(1)}, u32[]{:S(2)}, u32[]{:S(2)}) %collective-permute-start.3) | collective-permute-done | bytes 524320 | tf_op jit(solution)/shard_map/ppermute | solution.py:11
  136.7 1.1 bitcast_add_fusion
  (30 shorter events, 0.6 us)
Async XLA Ops:
  6.5 18.9 %copy-start = (s32[1,512]{1,0:T(1,128)S(1)}, s32[1,512]{1,0:T(1,128)}, u32[]{:S(2)}) copy-start(s32[1,512]{1,0:T(1,128)} %param.7) | copy-start | bytes 6148
  6.5 72.7 %copy-start.3 = (f32[1,2048,256]{2,1,0:T(8,128)S(1)}, f32[1,2048,256]{2,1,0:T(8,128)}, u32[]{:S(2)}) copy-start(f32[1,2048,256]{2,1,0:T(8,128)} %param.6) | copy-start | bytes 6291460
  6.5 93.2 %all-gather.4.cloned.1.call-start = ((), (), s32[]{:S(2)}) async-start(), calls=%async_computation.2 | async-start | bytes 4325376 | tf_op jit(solution)/shard_map/all_gather | solution.py:63
  10.2 49.2 %all-to-all-start = ((bf16[16,16,1024]{2,1,0:T(8,128)(2,1)}), bf16[16,16,1024]{2,1,0:T(8,128)(2,1)S(1)}, u32[]{:S(2)}, u32[]{:S(2)}) async-start(bf16[16,16,1024]{2,1,0:T(8,128)(2,1)} %stack.10), calls=%async_computation | async-start | bytes 1048576 | tf_op jit(solution)/shard_map/all_to_all | solution.py:58
  59.4 15.5 %collective-permute-start = (bf16[256,1024]{1,0:T(8,128)(2,1)S(1)}, bf16[256,1024]{1,0:T(8,128)(2,1)}, u32[]{:S(2)}, u32[]{:S(2)}) collective-permute-start(bf16[256,1024]{1,0:T(8,128)(2,1)S(1)} %bitcast.62), channel_id=1, source_target_pairs={{0,32},{32,64},{64,96},{96,0},{1,33},{33,65},{65,97},{97,1},{2,34}... | collective-permute-start | bytes 1572872 | tf_op jit(solution)/shard_map/ppermute | solution.py:28
  63.1 17.7 %collective-permute-start.2 = (bf16[256,1024]{1,0:T(8,128)(2,1)S(1)}, bf16[256,1024]{1,0:T(8,128)(2,1)}, u32[]{:S(2)}, u32[]{:S(2)}) collective-permute-start(bf16[256,1024]{1,0:T(8,128)(2,1)S(1)} %bitcast.63), channel_id=1, source_target_pairs={{0,96},{32,0},{64,32},{96,64},{1,97},{33,1},{65,33},{97,65},{2,98}... | collective-permute-start | bytes 1572872 | tf_op jit(solution)/shard_map/ppermute | solution.py:31
  74.9 11.4 %collective-permute-start.1 = (bf16[256,1024]{1,0:T(8,128)(2,1)}, bf16[256,1024]{1,0:T(8,128)(2,1)}, u32[]{:S(2)}, u32[]{:S(2)}) collective-permute-start(bf16[256,1024]{1,0:T(8,128)(2,1)} %collective-permute-done), channel_id=1, source_target_pairs={{0,32},{32,64},{64,96},{96,0},{1,33},{33,65},{65,97},{97,1},{2,34}... | collective-permute-start | bytes 1572872 | tf_op jit(solution)/shard_map/ppermute | solution.py:28
  102.7 13.7 %all-to-all-start.1 = ((bf16[4,64,1024]{2,1,0:T(8,128)(2,1)}), bf16[4,64,1024]{2,1,0:T(8,128)(2,1)S(1)}, u32[]{:S(2)}, u32[]{:S(2)}) async-start(bf16[4,64,1024]{2,1,0:T(8,128)(2,1)} %bitcast.16), calls=%async_computation.1 | async-start | bytes 1048576 | tf_op jit(solution)/shard_map/all_to_all | solution.py:95
  116.4 2.5 %copy-start.2 = (f32[1024,256]{1,0:T(8,128)S(1)}, f32[1024,256]{1,0:T(8,128)}, u32[]{:S(2)}) copy-start(f32[1024,256]{1,0:T(8,128)} %get-tuple-element.11) | copy-start | bytes 3145732
  121.0 3.6 %copy-start.1 = (f32[1024,256]{1,0:T(8,128)S(1)}, f32[1024,256]{1,0:T(8,128)}, u32[]{:S(2)}) copy-start(f32[1024,256]{1,0:T(8,128)} %get-tuple-element.9) | copy-start | bytes 3145732
  121.0 15.7 %collective-permute-start.3 = (bf16[1024,256]{1,0:T(8,128)(2,1)}, bf16[1024,256]{1,0:T(8,128)(2,1)S(1)}, u32[]{:S(2)}, u32[]{:S(2)}) collective-permute-start(bf16[1024,256]{1,0:T(8,128)(2,1)} %bitcast.65), channel_id=1, source_target_pairs={{0,128},{128,0},{256,384},{384,256},{1,129},{129,1},{257,385},{385... | collective-permute-start | bytes 1572872 | tf_op jit(solution)/shard_map/ppermute | solution.py:11
Sparse Core Ops, SparseCore 0:
  9.5 90.2 all-gather.3
